TPU v7x, 128 devices: a whole 4x4x4 slice. The times are simulated.
128 devices in a mesh: dp: 4 (over x), expert: 32 (over y, z, core).
Axes of the slice: x: 4, y: 4, z: 4, core: 2. Of those that a mesh axis runs over, the one named last changes fastest.
Arguments:
- tokens: bfloat16 [16384, 4096], P(('dp', 'expert')), may hold values from -6 to 6
- cotangent: bfloat16 [16384, 4096], P(('dp', 'expert')), may hold values from -6 to 6
- routes: int32 [16384], P(('dp', 'expert')), may hold values from 0 to 31, as said below
- combine: float32 [16384], P(('dp', 'expert')), may hold values from 0.05 to 1
- expert_weights: bfloat16 [32, 3, 1536, 4096], P('expert', None, 'dp'), may hold values from -0.09375 to 0.09375
Outputs:
- combined: bfloat16 [16384, 4096], P(('dp', 'expert'))
- token_grad: bfloat16 [16384, 4096], P(('dp', 'expert'))
- combine_grad: float32 [16384], P(('dp', 'expert'))
Inputs may be any that keep to these rules, and one draw needn't show every extreme that they name: `routes`: among the 128 rows of every device, two experts, the same two on every device, are each named by exactly 8 rows, and every other expert by 3 or 4 rows.
All inputs are finite; a program needn't handle non-finite values.
Results may differ from a plain program's by a relative error of at most 0.015.
Values may be sent and summed in bfloat16 or wider, within the bound.
No kernel may reach another device: no remote copies, remote signals or barrier semaphores. Data moves between devices by JAX's collectives and lax.ppermute only.
A program may use at most 192 MiB of HBM per device.

v0:
```python
import jax
import jax.numpy as jnp
from jax import lax
from jax.sharding import PartitionSpec as P


def placement(member, slot_count):
    within = jnp.sum((jnp.cumsum(member, 0) - 1) * member, 1)
    owner_group = jnp.sum(member * lax.iota(jnp.int32, member.shape[1])[None, :], 1)
    is_used = jnp.sum(member, 1) > 0
    target = owner_group * slot_count + within
    buffer_cells = lax.iota(jnp.int32, member.shape[1] * slot_count)
    return ((buffer_cells[:, None] == target[None, :]) & is_used[None, :]).astype(jnp.bfloat16)


def spread(layout, row_block):
    return jnp.dot(layout, row_block, preferred_element_type=jnp.float32).astype(jnp.bfloat16)


def collect(layout, buffer_rows):
    return lax.dot_general(
        layout, buffer_rows, (((0,), (0,)), ((), ())), preferred_element_type=jnp.float32
    )


def group_rows(values):
    return lax.all_gather(values, "dp", axis=0, tiled=True)


def group_sum(values):
    return lax.psum_scatter(
        values.astype(jnp.bfloat16), "dp", scatter_dimension=0, tiled=True
    ).astype(jnp.float32)


def send_rows(cold_buf, experts, slot_count, model_width):
    arrived = lax.all_to_all(
        cold_buf.reshape(experts, slot_count, model_width),
        "expert",
        split_axis=0,
        concat_axis=0,
        tiled=True,
    ).reshape(-1, model_width)
    cold_in = group_rows(arrived)
    hot_in = None
    return (cold_in, hot_in)


def return_rows(cold_part, experts, slot_count, model_width):
    cold_total = group_sum(cold_part)
    hot_out = None
    summed = cold_total.astype(jnp.bfloat16).reshape(experts, slot_count, model_width)
    cold_out = lax.all_to_all(summed, "expert", split_axis=0, concat_axis=0, tiled=True).reshape(
        -1, model_width
    )
    return (cold_out, hot_out)


def forward_rows(row_block, matrices):
    gate_up = jnp.einsum("rd,kfd->krf", row_block, matrices[:2], preferred_element_type=jnp.float32)
    gate_act = gate_up[0]
    up_act = gate_up[1]
    hidden = (gate_act * jax.nn.sigmoid(gate_act) * up_act).astype(jnp.bfloat16)
    partial_out = jnp.dot(hidden, matrices[2], preferred_element_type=jnp.float32)
    return (gate_act, up_act, partial_out)


def backward_rows(row_block, gate_act, up_act, matrices):
    hidden_grad = lax.dot_general(
        row_block, matrices[2], (((1,), (1,)), ((), ())), preferred_element_type=jnp.float32
    )
    squashed = jax.nn.sigmoid(gate_act)
    gate_grad = (hidden_grad * up_act * squashed * (1.0 + gate_act * (1.0 - squashed))).astype(
        jnp.bfloat16
    )
    up_grad = (hidden_grad * gate_act * squashed).astype(jnp.bfloat16)
    both_grads = jnp.stack([gate_grad, up_grad])
    return jnp.einsum("krf,kfd->rd", both_grads, matrices[:2], preferred_element_type=jnp.float32)


def shards(tokens, cotangent, routes, combine, expert_weights):
    weights = expert_weights[0]
    tok_dev = tokens.shape[0]
    model_width = tokens.shape[1]
    experts = lax.axis_size("expert")
    capacity = 2 * tok_dev // experts
    labels = lax.iota(jnp.int32, experts)
    member = (routes[:, None] == labels[None, :]).astype(jnp.int32)
    cold_layout = placement(member, capacity)
    cold_buf = spread(cold_layout, tokens)
    cold_in, hot_in = send_rows(cold_buf, experts, capacity, model_width)
    gate_act, up_act, cold_part = forward_rows(cold_in, weights)
    cold_out, hot_out = return_rows(cold_part, experts, capacity, model_width)
    expert_out = collect(cold_layout, cold_out)
    cotangent_wide = cotangent.astype(jnp.float32)
    combined = (combine[:, None] * expert_out).astype(jnp.bfloat16)
    combine_grad = jnp.sum(expert_out * cotangent_wide, 1)
    out_grad = (combine[:, None] * cotangent_wide).astype(jnp.bfloat16)
    cold_grad_buf = spread(cold_layout, out_grad)
    cold_grad_in, hot_grad_in = send_rows(cold_grad_buf, experts, capacity, model_width)
    cold_grad_part = backward_rows(cold_grad_in, gate_act, up_act, weights)
    cold_grad_out, hot_grad_out = return_rows(cold_grad_part, experts, capacity, model_width)
    input_grad = collect(cold_layout, cold_grad_out)
    token_grad = input_grad.astype(jnp.bfloat16)
    return (combined, token_grad, combine_grad)


def solution(mesh):
    return jax.shard_map(
        shards,
        mesh=mesh,
        in_specs=(
            P(("dp", "expert"), None),
            P(("dp", "expert"), None),
            P(("dp", "expert")),
            P(("dp", "expert")),
            P("expert", None, "dp", None),
        ),
        out_specs=(P(("dp", "expert"), None), P(("dp", "expert"), None), P(("dp", "expert"))),
        check_vma=False,
    )
```

profile of v0, /device:TPU:1, one launch (start us, length us, event | category | flops | bytes accessed | tf_op | source)
XLA Modules:
  0.0 446.6 jit_solution(15779998642776179402)
XLA Ops:
  7.2 0.8 fusion.49
  8.1 0.2 reduce_window_sum.11
  8.2 0.9 fusion.54
  9.1 0.7 fusion.6
  9.8 37.7 %all_to_all.20 = bf16[32,8,4096]{2,1,0:T(8,128)(2,1)} all-to-all(bf16[32,8,4096]{2,1,0:T(8,128)(2,1)S(1)} %fusion.6), channel_id=1, replica_groups=mesh['dp'=4,'expert'=32] {'expert'}, dimensions={0} | all-to-all | bytes 4194304 | tf_op jit(solution)/shard_map/all_to_all | solution.py:37
  47.5 0.0 all-gather.5.cloned.1.call-start
  47.6 1.1 copy-done.2
  48.7 0.8 fusion.7
  49.5 32.0 %all_to_all.21 = bf16[32,8,4096]{2,1,0:T(8,128)(2,1)} all-to-all(bf16[32,8,4096]{2,1,0:T(8,128)(2,1)S(1)} %fusion.7), channel_id=1, replica_groups=mesh['dp'=4,'expert'=32] {'expert'}, dimensions={0} | all-to-all | bytes 4194304 | tf_op jit(solution)/shard_map/all_to_all | solution.py:37
  81.5 0.0 reduce-scatter.5.cloned.1.call-start
  81.6 46.7 %all-gather.3.cloned.1.call-done = bf16[1024,4096]{1,0:T(8,128)(2,1)} async-done(((bf16[256,4096]{1,0:T(8,128)(2,1)}), bf16[1024,4096]{1,0:T(8,128)(2,1)}) %all-gather.3.cloned.1.call-update) | async-done | bytes 8388624 | tf_op jit(solution)/shard_map/all_gather | solution.py:27
  128.3 12.1 %fusion.18 = f32[2,1024,384]{2,1,0:T(8,128)} fusion(bf16[1,3,384,4096]{3,2,1,0:T(8,128)(2,1)} %param.9, bf16[1024,4096]{1,0:T(8,128)(2,1)} %all-gather.3.cloned.1.call-done), kind=kOutput, calls=%fused_computation.26 | convolution fusion | flops 6442450944 | bytes 17825792 | tf_op jit(solution)/shard_map/rd,kfd->krf/dot_general | solution.py:60
  140.5 73.6 %all-gather.5.cloned.1.call-done = bf16[1024,4096]{1,0:T(8,128)(2,1)} async-done(((bf16[256,4096]{1,0:T(8,128)(2,1)}), bf16[1024,4096]{1,0:T(8,128)(2,1)}) %all-gather.5.cloned.1.call-update) | async-done | bytes 8388624 | tf_op jit(solution)/shard_map/all_gather | solution.py:27
  214.1 10.1 %fusion.39 = (bf16[1,1024,384]{2,1,0:T(8,128)(2,1)S(1)}, bf16[1,1024,384]{2,1,0:T(8,128)(2,1)S(1)}) fusion(f32[2,1024,384]{2,1,0:T(8,128)} %fusion.18, bf16[1024,4096]{1,0:T(8,128)(2,1)} %all-gather.5.cloned.1.call-done, bf16[1,3,384,4096]{3,2,1,0:T(8,128)(2,1)} %param.9), kind=kOutput, calls=%fused_computation.47 | convolution fusion | flops 3226337280 | bytes 16252928 | tf_op jit(solution)/shard_map/dot_general | solution.py:69
  224.2 11.5 %bitcast_convert_fusion = bf16[1024,4096]{1,0:T(8,128)(2,1)} fusion(bf16[1,3,384,4096]{3,2,1,0:T(8,128)(2,1)} %param.9, bf16[1,1024,384]{2,1,0:T(8,128)(2,1)S(1)} %get-tuple-element.7, bf16[1,1024,384]{2,1,0:T(8,128)(2,1)S(1)} %get-tuple-element.6), kind=kOutput, calls=%fused_computation | convolution fusion | flops 6447431680 | bytes 16252928 | tf_op jit(solution)/shard_map/krf,kfd->rd/dot_general | solution.py:78
  235.7 0.2 reduce-scatter.3.cloned.1.call-start
  235.9 11.0 %convolution_convert_fusion = bf16[1024,4096]{1,0:T(8,128)(2,1)} fusion(bf16[1,3,384,4096]{3,2,1,0:T(8,128)(2,1)} %param.9, f32[2,1024,384]{2,1,0:T(8,128)} %fusion.18), kind=kOutput, calls=%fused_computation.3 | convolution fusion | flops 3227779072 | bytes 14680064 | tf_op jit(solution)/shard_map/dot_general | solution.py:64
  246.9 70.4 %reduce-scatter.5.cloned.1.call-done = bf16[256,4096]{1,0:T(8,128)(2,1)} async-done(((bf16[1024,4096]{1,0:T(8,128)(2,1)}), bf16[256,4096]{1,0:T(8,128)(2,1)}) %reduce-scatter.5.cloned.1.call-update) | async-done | bytes 2097168 | tf_op jit(solution)/shard_map/reduce_scatter | solution.py:31
  317.4 7.6 %all-to-all-start.3 = ((bf16[32,8,4096]{2,1,0:T(8,128)(2,1)}), bf16[32,8,4096]{2,1,0:T(8,128)(2,1)S(1)}, u32[]{:S(2)}, u32[]{:S(2)}) async-start(bf16[32,8,4096]{2,1,0:T(8,128)(2,1)} %bitcast.86), calls=%async_computation.5 | async-start | bytes 4194304 | tf_op jit(solution)/shard_map/all_to_all | solution.py:53
  325.0 74.9 %reduce-scatter.3.cloned.1.call-done = bf16[256,4096]{1,0:T(8,128)(2,1)} async-done(((bf16[1024,4096]{1,0:T(8,128)(2,1)}), bf16[256,4096]{1,0:T(8,128)(2,1)}) %reduce-scatter.3.cloned.1.call-update) | async-done | bytes 2097168 | tf_op jit(solution)/shard_map/reduce_scatter | solution.py:31
  399.9 7.7 %all-to-all-start.1 = ((bf16[32,8,4096]{2,1,0:T(8,128)(2,1)}), bf16[32,8,4096]{2,1,0:T(8,128)(2,1)}, u32[]{:S(2)}, u32[]{:S(2)}) async-start(bf16[32,8,4096]{2,1,0:T(8,128)(2,1)} %bitcast.87), calls=%async_computation.2 | async-start | bytes 4194304 | tf_op jit(solution)/shard_map/all_to_all | solution.py:53
  407.6 1.5 convolution_convert_fusion.3
  409.1 26.9 %all-to-all-done.1 = bf16[32,8,4096]{2,1,0:T(8,128)(2,1)} async-done(((bf16[32,8,4096]{2,1,0:T(8,128)(2,1)}), bf16[32,8,4096]{2,1,0:T(8,128)(2,1)}, u32[]{:S(2)}, u32[]{:S(2)}) %all-to-all-start.1) | async-done | bytes 2097184 | tf_op jit(solution)/shard_map/all_to_all | solution.py:53
  436.0 4.1 fusion.14
  (15 shorter events, 0.1 us)
Async XLA Ops:
  7.2 2.0 copy-start
  7.2 121.1 %all-gather.3.cloned.1.call-start = ((), (), s32[]{:S(2)}) async-start(), calls=%async_computation.6 | async-start | bytes 10485760 | tf_op jit(solution)/shard_map/all_gather | solution.py:27
  47.5 1.2 copy-start.2
  47.5 1.2 copy-start.3
  47.5 166.6 %all-gather.5.cloned.1.call-start = ((), (), s32[]{:S(2)}) async-start(), calls=%async_computation.8 | async-start | bytes 10485760 | tf_op jit(solution)/shard_map/all_gather | solution.py:27
  81.5 235.8 %reduce-scatter.5.cloned.1.call-start = ((), (), s32[]{:S(2)}) async-start(), calls=%async_computation.9 | async-start | bytes 10485760 | tf_op jit(solution)/shard_map/reduce_scatter | solution.py:31
  235.7 164.2 %reduce-scatter.3.cloned.1.call-start = ((), (), s32[]{:S(2)}) async-start(), calls=%async_computation.7 | async-start | bytes 10485760 | tf_op jit(solution)/shard_map/reduce_scatter | solution.py:31
  317.4 82.6 %all-to-all-start.3 = ((bf16[32,8,4096]{2,1,0:T(8,128)(2,1)}), bf16[32,8,4096]{2,1,0:T(8,128)(2,1)S(1)}, u32[]{:S(2)}, u32[]{:S(2)}) async-start(bf16[32,8,4096]{2,1,0:T(8,128)(2,1)} %bitcast.86), calls=%async_computation.5 | async-start | bytes 4194304 | tf_op jit(solution)/shard_map/all_to_all | solution.py:53
  399.9 36.1 %all-to-all-start.1 = ((bf16[32,8,4096]{2,1,0:T(8,128)(2,1)}), bf16[32,8,4096]{2,1,0:T(8,128)(2,1)}, u32[]{:S(2)}, u32[]{:S(2)}) async-start(bf16[32,8,4096]{2,1,0:T(8,128)(2,1)} %bitcast.87), calls=%async_computation.2 | async-start | bytes 4194304 | tf_op jit(solution)/shard_map/all_to_all | solution.py:53
  407.6 32.4 %copy-start.1 = (bf16[128,4096]{1,0:T(8,128)(2,1)S(1)}, bf16[128,4096]{1,0:T(8,128)(2,1)}, u32[]{:S(2)}) copy-start(bf16[128,4096]{1,0:T(8,128)(2,1)} %param.5) | copy-start | bytes 3145732
Sparse Core Ops, SparseCore 0:
  47.6 80.6 all-gather.2
  130.0 84.0 all-gather.4
  235.8 81.4 reduce-scatter.4
  319.7 80.1 reduce-scatter.2
where the time goes:
time: 447 us
  waiting for transfers between devices  293 us (66%)
  blocking collectives  69.7 us (16%)
  matrix products  51.7 us (12%)
  starting transfers between devices  15.7 us (4%)
  between operations  13.9 us (3%)
    reduce_scatter x2, waiting for transfers between devices, group_sum(): lax.psum_scatter(values.astype(jnp.bfloat16), 'dp', scatter_dimension=0,...  145 us
    all_gather x2, waiting for transfers between devices, group_rows(): return lax.all_gather(values, 'dp', axis=0, tiled=True)  120 us
    all_to_all x2, blocking collectives, send_rows(): lax.all_to_all(cold_buf.reshape(experts, slot_count, model_width), 'exper...  69.7 us
    all_to_all x2, waiting for transfers between devices, return_rows(): lax.all_to_all(summed, 'expert', split_axis=0, concat_axis=0, tiled=True)  26.9 us
    all_to_all x2, starting transfers between devices, return_rows(): lax.all_to_all(summed, 'expert', split_axis=0, concat_axis=0, tiled=True)  15.3 us
    dot_general x1, matrix products, forward_rows(): jnp.einsum('rd,kfd->krf', row_block, matrices[:2], preferred_element_type...  12.1 us
    dot_general x1, matrix products, backward_rows(): jnp.einsum('krf,kfd->rd', both_grads, matrices[:2], preferred_element_typ...  11.5 us
    dot_general x1, matrix products, forward_rows(): jnp.dot(hidden, matrices[2], preferred_element_type=jnp.float32)  11 us
  transfers between devices with their start and end apart: 6, of which 5 were waited for; matrix products, arithmetic and copies ran while one was open for 6% of the time, Pallas kernels for 0%

commit v1 on v0

--- a/solution.py
+++ b/solution.py
@@ -24,7 +24,16 @@
 
 
 def group_rows(values):
-    return lax.all_gather(values, "dp", axis=0, tiled=True)
+    scan_ladders = lambda message, bus_axis: jnp.concatenate(
+        jax.lax.all_to_all(
+            jnp.stack(jax.lax.axis_size(bus_axis) * [message], 0),
+            axis_name=bus_axis,
+            split_axis=0,
+            concat_axis=0,
+        ),
+        0,
+    )
+    return scan_ladders(values, bus_axis="dp")
 
 
 def group_sum(values):

time: 447 us -> 476 us (1.065)
  blocking collectives: 69.7 us -> 298 us
  waiting for transfers between devices: 293 us -> 97.2 us
  matrix products: 51.7 us -> 43.9 us
    all_to_all x0 -> x2, blocking collectives: none -> 228 us  [group_rows(): jax.lax.all_to_all(jnp.stack(jax.lax.axis_size(bus_axis) * [message], 0),...]
    all_gather x2 -> x0, waiting for transfers between devices: 120 us -> none  [group_rows(): return lax.all_gather(values, 'dp', axis=0, tiled=True)]
    reduce_scatter x2, waiting for transfers between devices: 145 us -> 72.4 us  [group_sum(): lax.psum_scatter(values.astype(jnp.bfloat16), 'dp', scatter_dimension=0,...]
  transfers between devices with their start and end apart: 6 -> 4, of which waited for: 5 -> 2; matrix products, arithmetic and copies ran while one was open for 6% -> 5% of each run, Pallas kernels for 0% -> 0%
where the time goes in v1:
time: 476 us; the launch traced here: 475 us
  blocking collectives  298 us (63%)
  waiting for transfers between devices  97.2 us (20%)
  matrix products  43.9 us (9%)
  starting transfers between devices  15.4 us (3%)
  between operations  14.2 us (3%)
  local copies, waits for them, and re-layouts  5.01 us (1%)
    all_to_all x2, blocking collectives, group_rows(): jax.lax.all_to_all(jnp.stack(jax.lax.axis_size(bus_axis) * [message], 0),...  228 us
    reduce_scatter x2, waiting for transfers between devices, group_sum(): lax.psum_scatter(values.astype(jnp.bfloat16), 'dp', scatter_dimension=0,...  72.4 us
    all_to_all x2, blocking collectives, send_rows(): lax.all_to_all(cold_buf.reshape(experts, slot_count, model_width), 'exper...  70.3 us
    all_to_all x2, waiting for transfers between devices, return_rows(): lax.all_to_all(summed, 'expert', split_axis=0, concat_axis=0, tiled=True)  24.7 us
    all_to_all x2, starting transfers between devices, return_rows(): lax.all_to_all(summed, 'expert', split_axis=0, concat_axis=0, tiled=True)  15.3 us
    dot_general x1, matrix products, forward_rows(): jnp.einsum('rd,kfd->krf', row_block, matrices[:2], preferred_element_type...  11 us
  transfers between devices with their start and end apart: 4, of which 2 were waited for; matrix products, arithmetic and copies ran while one was open for 5% of the time, Pallas kernels for 0%

profile of v1, /device:TPU:1, one launch (start us, length us, event | category | flops | bytes accessed | tf_op | source)
XLA Modules:
  0.0 475.4 jit_solution(17632065826538604843)
XLA Ops:
  7.2 0.8 fusion.46
  8.1 0.2 reduce_window_sum.11
  8.2 0.9 fusion.51
  9.1 0.7 fusion.5
  9.8 37.6 %all_to_all.30 = bf16[32,8,4096]{2,1,0:T(8,128)(2,1)S(1)} all-to-all(bf16[32,8,4096]{2,1,0:T(8,128)(2,1)S(1)} %fusion.5), channel_id=1, replica_groups=mesh['dp'=4,'expert'=32] {'expert'}, dimensions={0} | all-to-all | bytes 4194304 | tf_op jit(solution)/shard_map/all_to_all | solution.py:46
  47.4 1.0 stack.15
  48.4 97.2 %all_to_all.31 = bf16[4,256,4096]{2,1,0:T(8,128)(2,1)S(1)} all-to-all(bf16[4,256,4096]{2,1,0:T(8,128)(2,1)S(1)} %stack.15), channel_id=1, replica_groups=mesh['dp'=4,'expert'=32] {'dp'}, dimensions={0} | all-to-all | bytes 16777216 | tf_op jit(solution)/shard_map/all_to_all | solution.py:28
  145.7 11.0 %fusion.17 = f32[2,1024,384]{2,1,0:T(8,128)S(1)} fusion(bf16[1024,4096,1]{1,0,2:T(8,128)(2,1)S(1)} %bitcast.87, bf16[1,3,384,4096]{3,2,1,0:T(8,128)(2,1)} %param.9), kind=kOutput, calls=%fused_computation.25 | convolution fusion | flops 6442450944 | bytes 17825792 | tf_op jit(solution)/shard_map/rd,kfd->krf/dot_general | solution.py:69
  156.6 1.7 copy-done.4
  158.4 8.6 %convolution_convert_fusion = bf16[1024,4096]{1,0:T(8,128)(2,1)} fusion(bf16[1,3,384,4096]{3,2,1,0:T(8,128)(2,1)} %param.9, f32[2,1024,384]{2,1,0:T(8,128)S(1)} %fusion.17), kind=kOutput, calls=%fused_computation.1 | convolution fusion | flops 3227779072 | bytes 14680064 | tf_op jit(solution)/shard_map/dot_general | solution.py:73
  167.0 0.0 reduce-scatter.5.cloned.1.call-start
  167.1 1.1 copy-done.2
  168.2 0.8 fusion.6
  169.0 32.7 %all_to_all.32 = bf16[32,8,4096]{2,1,0:T(8,128)(2,1)S(1)} all-to-all(bf16[32,8,4096]{2,1,0:T(8,128)(2,1)S(1)} %fusion.6), channel_id=1, replica_groups=mesh['dp'=4,'expert'=32] {'expert'}, dimensions={0} | all-to-all | bytes 4194304 | tf_op jit(solution)/shard_map/all_to_all | solution.py:46
  201.7 1.0 stack.16
  202.8 130.3 %all_to_all.33 = bf16[4,256,4096]{2,1,0:T(8,128)(2,1)S(1)} all-to-all(bf16[4,256,4096]{2,1,0:T(8,128)(2,1)S(1)} %stack.16), channel_id=1, replica_groups=mesh['dp'=4,'expert'=32] {'dp'}, dimensions={0} | all-to-all | bytes 16777216 | tf_op jit(solution)/shard_map/all_to_all | solution.py:28
  333.1 7.5 %fusion.36 = (bf16[1,1024,384]{2,1,0:T(8,128)(2,1)S(1)}, bf16[1,1024,384]{2,1,0:T(8,128)(2,1)S(1)}) fusion(f32[2,1024,384]{2,1,0:T(8,128)} %copy-done.4, bf16[1024,4096]{1,0:T(8,128)(2,1)S(1)} %bitcast.86, bf16[1,3,384,4096]{3,2,1,0:T(8,128)(2,1)} %param.9), kind=kOutput, calls=%fused_computation.46 | convolution fusion | flops 3226337280 | bytes 16252928 | tf_op jit(solution)/shard_map/dot_general | solution.py:78
  340.7 8.6 %bitcast_convert_fusion = bf16[1024,4096]{1,0:T(8,128)(2,1)} fusion(bf16[1,3,384,4096]{3,2,1,0:T(8,128)(2,1)S(1)} %bitcast.91, bf16[1,1024,384]{2,1,0:T(8,128)(2,1)S(1)} %get-tuple-element.7, bf16[1,1024,384]{2,1,0:T(8,128)(2,1)S(1)} %get-tuple-element.6), kind=kOutput, calls=%fused_computation | convolution fusion | flops 6447431680 | bytes 16252928 | tf_op jit(solution)/shard_map/krf,kfd->rd/dot_general | solution.py:87
  349.4 7.6 %all-to-all-start.2 = ((bf16[32,8,4096]{2,1,0:T(8,128)(2,1)}), bf16[32,8,4096]{2,1,0:T(8,128)(2,1)S(1)}, u32[]{:S(2)}, u32[]{:S(2)}) async-start(bf16[32,8,4096]{2,1,0:T(8,128)(2,1)} %bitcast.88), calls=%async_computation.3 | async-start | bytes 4194304 | tf_op jit(solution)/shard_map/all_to_all | solution.py:62
  357.0 72.4 %reduce-scatter.5.cloned.1.call-done = bf16[256,4096]{1,0:T(8,128)(2,1)} async-done(((bf16[1024,4096]{1,0:T(8,128)(2,1)}), bf16[256,4096]{1,0:T(8,128)(2,1)}) %reduce-scatter.5.cloned.1.call-update) | async-done | bytes 2097168 | tf_op jit(solution)/shard_map/reduce_scatter | solution.py:40
  429.4 7.7 %all-to-all-start.5 = ((bf16[32,8,4096]{2,1,0:T(8,128)(2,1)}), bf16[32,8,4096]{2,1,0:T(8,128)(2,1)}, u32[]{:S(2)}, u32[]{:S(2)}) async-start(bf16[32,8,4096]{2,1,0:T(8,128)(2,1)} %bitcast.89), calls=%async_computation.7 | async-start | bytes 4194304 | tf_op jit(solution)/shard_map/all_to_all | solution.py:62
  437.1 3.6 fusion.13
  440.7 24.7 %all-to-all-done.5 = bf16[32,8,4096]{2,1,0:T(8,128)(2,1)} async-done(((bf16[32,8,4096]{2,1,0:T(8,128)(2,1)}), bf16[32,8,4096]{2,1,0:T(8,128)(2,1)}, u32[]{:S(2)}, u32[]{:S(2)}) %all-to-all-start.5) | async-done | bytes 2097184 | tf_op jit(solution)/shard_map/all_to_all | solution.py:62
  465.5 3.1 convolution_convert_fusion.3
  (22 shorter events, 0.1 us)
Async XLA Ops:
  7.2 2.0 copy-start
  7.2 342.2 %reduce-scatter.3.cloned.1.call-start = ((), (), s32[]{:S(2)}) async-start(), calls=%async_computation.8 | async-start | bytes 10485760 | tf_op jit(solution)/shard_map/reduce_scatter | solution.py:40
  156.6 1.7 copy-start.4
  167.0 1.2 copy-start.2
  167.0 1.2 copy-start.3
  167.0 262.4 %reduce-scatter.5.cloned.1.call-start = ((), (), s32[]{:S(2)}) async-start(), calls=%async_computation.9 | async-start | bytes 10485760 | tf_op jit(solution)/shard_map/reduce_scatter | solution.py:40
  202.8 137.9 %slice-start = ((s8[9437184]{0:T(1024)(128)(4,1)}), s8[4194304]{0:T(1024)(128)(4,1)S(1)}, s32[]{:S(2)}) async-start(s8[9437184]{0:T(1024)(128)(4,1)} %bitcast.90), calls=%async_computation.10 | async-start | bytes 8388608
  333.1 7.6 %slice-start.1 = ((s8[9437184]{0:T(1024)(128)(4,1)}), s8[4194304]{0:T(1024)(128)(4,1)S(1)}, s32[]{:S(2)}) async-start(s8[9437184]{0:T(1024)(128)(4,1)} %bitcast.90), calls=%async_computation.11 | async-start | bytes 8388608
  333.1 7.6 %slice-start.2 = ((s8[9437184]{0:T(1024)(128)(4,1)}), s8[1048576]{0:T(1024)(128)(4,1)S(1)}, s32[]{:S(2)}) async-start(s8[9437184]{0:T(1024)(128)(4,1)} %bitcast.90), calls=%async_computation.12 | async-start | bytes 2097152
  349.4 80.0 %all-to-all-start.2 = ((bf16[32,8,4096]{2,1,0:T(8,128)(2,1)}), bf16[32,8,4096]{2,1,0:T(8,128)(2,1)S(1)}, u32[]{:S(2)}, u32[]{:S(2)}) async-start(bf16[32,8,4096]{2,1,0:T(8,128)(2,1)} %bitcast.88), calls=%async_computation.3 | async-start | bytes 4194304 | tf_op jit(solution)/shard_map/all_to_all | solution.py:62
  429.4 36.1 %all-to-all-start.5 = ((bf16[32,8,4096]{2,1,0:T(8,128)(2,1)}), bf16[32,8,4096]{2,1,0:T(8,128)(2,1)}, u32[]{:S(2)}, u32[]{:S(2)}) async-start(bf16[32,8,4096]{2,1,0:T(8,128)(2,1)} %bitcast.89), calls=%async_computation.7 | async-start | bytes 4194304 | tf_op jit(solution)/shard_map/all_to_all | solution.py:62
  437.1 31.4 %copy-start.1 = (bf16[128,4096]{1,0:T(8,128)(2,1)S(1)}, bf16[128,4096]{1,0:T(8,128)(2,1)}, u32[]{:S(2)}) copy-start(bf16[128,4096]{1,0:T(8,128)(2,1)} %param.5) | copy-start | bytes 3145732
Sparse Core Ops, SparseCore 0:
  167.1 141.5 reduce-scatter.2
  349.5 79.8 reduce-scatter.4
